TPU v7x, 32 devices: a whole 2x2x4 slice. The times are simulated.
32 devices in a mesh: dp: 8 (over z, core), rot: 4 (over y, x).
Axes of the slice: x: 2, y: 2, z: 4, core: 2. Of those that a mesh axis runs over, the one named last changes fastest.
Arguments:
- vectors: bfloat16 [2048, 4096], P('dp', 'rot'), may hold values from -100 to 100
- rotation: bfloat16 [4096, 4096], P('rot'), may hold values from -0.125 to 0.125
- codes: int32 [2048, 256], P('dp', 'rot'), may hold values from 0 to 255
Outputs:
- codebook: float32 [4096, 256], P('rot')
- new_rotation: bfloat16 [4096, 4096], P('rot', 'dp')
All inputs are finite; a program needn't handle non-finite values.
Results may differ from a plain program's by a relative error of at most 0.007.
Values may be sent and summed in bfloat16 or wider, within the bound.
No kernel may reach another device: no remote copies, remote signals or barrier semaphores. Data moves between devices by JAX's collectives and lax.ppermute only.
A program may use at most 64 MiB of HBM per device.

v0:
```python
import math
import jax
import jax.numpy as jnp
from jax import lax
from jax.sharding import PartitionSpec as P

K = 256
ITERS = 2


def body(vectors, rotation, codes):
    row_count, block_dims = vectors.shape
    width = rotation.shape[1]
    local_spaces = codes.shape[1]
    sub_dims = block_dims // local_spaces
    tile_cols = width // lax.axis_size("dp")
    tile_spaces = tile_cols // sub_dims
    dp_index = lax.axis_index("dp")
    code_ids = jnp.arange(K, dtype=jnp.int32)
    dp_size = lax.axis_size("dp")
    row_codes = lax.all_gather(codes, "rot", axis=1, tiled=True)

    def block_codes(block):
        return lax.dynamic_slice_in_dim(row_codes, block * tile_spaces, tile_spaces, 1).astype(
            jnp.bfloat16
        )

    if dp_size % 2:
        parts = [jnp.concatenate([vectors, block_codes(dp_index)], axis=1)]
        for shift in range(1, dp_size):
            pairs = [(i, (i + shift) % dp_size) for i in range(dp_size)]
            target = (dp_index + shift) % dp_size
            parts.append(
                lax.ppermute(jnp.concatenate([vectors, block_codes(target)], axis=1), "dp", pairs)
            )
        joined = jnp.concatenate(parts, axis=0)
    else:

        def pair_part(block):
            return jnp.concatenate([vectors, block_codes(block), block_codes(block ^ 1)], axis=1)

        parts = [pair_part(dp_index)]
        for shift in range(2, dp_size, 2):
            pairs = [(i, (i + shift) % dp_size) for i in range(dp_size)]
            parts.append(lax.ppermute(pair_part((dp_index + shift) % dp_size), "dp", pairs))
        group = jnp.concatenate(parts, axis=0)
        mine = group[:, : block_dims + tile_spaces]
        for_mate = jnp.concatenate(
            [group[:, :block_dims], group[:, block_dims + tile_spaces :]], axis=1
        )
        mates = [(i, i ^ 1) for i in range(dp_size)]
        joined = jnp.concatenate([mine, lax.ppermute(for_mate, "dp", mates)], axis=0)
    all_vectors = joined[:, :block_dims]
    tile_codes = joined[:, block_dims:].astype(jnp.int32)
    rotated_t = lax.psum_scatter(
        lax.dot_general(
            rotation, vectors, (((0,), (1,)), ((), ())), preferred_element_type=jnp.float32
        ),
        "rot",
        scatter_dimension=0,
        tiled=True,
    ).astype(jnp.bfloat16)
    code_indicator = (codes.T[:, :, None] == code_ids[None, None, :]).astype(jnp.bfloat16)
    grouped_vectors = rotated_t.reshape(local_spaces, sub_dims, row_count)
    shard_code_sums = jnp.einsum(
        "vzo,voc->vzc", grouped_vectors, code_indicator, preferred_element_type=jnp.float32
    )
    local_counts = jnp.sum(code_indicator, axis=1, dtype=jnp.float32)
    total_sums, total_counts = lax.psum((shard_code_sums, local_counts), "dp")
    book = total_sums / jnp.maximum(total_counts, 1.0)[:, None, :]
    codebook = book.reshape(block_dims, K)
    blocks_per_rot = local_spaces // tile_spaces
    offered = lax.dynamic_slice_in_dim(
        book.astype(jnp.bfloat16), dp_index % blocks_per_rot * tile_spaces, tile_spaces, 0
    )
    tile_book = lax.all_gather(offered, "rot", axis=0)[dp_index // blocks_per_rot]
    tile_book, all_vectors, tile_codes = lax.optimization_barrier(
        (tile_book, all_vectors, tile_codes)
    )
    tile_indicator = (tile_codes.T[:, :, None] == code_ids[None, None, :]).astype(jnp.bfloat16)
    rebuilt_t = jnp.einsum(
        "lyg,lxg->lyx", tile_book, tile_indicator, preferred_element_type=jnp.float32
    )
    rebuilt_t = rebuilt_t.astype(jnp.bfloat16).reshape(tile_cols, all_vectors.shape[0])
    cross_tile = lax.dot_general(
        all_vectors, rebuilt_t, (((0,), (1,)), ((), ())), preferred_element_type=jnp.float32
    ).astype(jnp.bfloat16)

    def apply_gram(rows_b, gram_b):
        return jnp.dot(
            rows_b,
            lax.all_gather(gram_b, "rot", axis=0, tiled=True),
            preferred_element_type=jnp.float32,
        )

    columns = cross_tile
    new_tile = None
    for iteration in range(ITERS):
        rows_b = lax.all_gather(columns, "dp", axis=1, tiled=True)
        partial = lax.dot_general(
            rows_b, columns, (((0,), (0,)), ((), ())), preferred_element_type=jnp.float32
        ).astype(jnp.bfloat16)
        if iteration == 0:
            gram_part = lax.psum_scatter(partial, "rot", scatter_dimension=0, tiled=True)
        else:
            gram_part = lax.psum(partial, "rot")
        if iteration == 0:
            gram_f = gram_part.astype(jnp.float32)
            total = lax.psum(jnp.sum(gram_f * gram_f), ("dp", "rot"))
            factor = 1.7 / jnp.sqrt(jnp.sqrt(total))
            product = apply_gram(rows_b, gram_part)
            new_tile = factor * (
                1.5 * columns.astype(jnp.float32) - 0.5 * (factor * factor) * product
            )
        else:
            product = jnp.dot(rows_b, gram_part, preferred_element_type=jnp.float32)
            new_tile = 1.5 * columns.astype(jnp.float32) - 0.5 * product
        columns = new_tile.astype(jnp.bfloat16)
    new_rotation = (math.sqrt(width) * new_tile).astype(jnp.bfloat16)
    return (codebook, new_rotation)


def solution(mesh):
    return jax.shard_map(
        body,
        mesh=mesh,
        in_specs=(P("dp", "rot"), P("rot", None), P("dp", "rot")),
        out_specs=(P("rot", None), P("rot", "dp")),
        check_vma=False,
    )
```

profile of v0, /device:TPU:0, one launch (start us, length us, event | category | flops | bytes accessed | tf_op | source)
XLA Modules:
  0.0 616.0 jit_solution(11668680264245755234)
XLA Ops:
  7.2 0.0 reduce-scatter.3.cloned.1.call-start
  7.2 7.8 %fusion.19 = f32[4096,256]{1,0:T(8,128)} fusion(bf16[1024,4096]{1,0:T(8,128)(2,1)} %param.4, bf16[256,1024]{1,0:T(8,128)(2,1)} %param.3), kind=kOutput, calls=%fused_computation.48 | convolution fusion | flops 2147483648 | bytes 13107200 | tf_op jit(solution)/shard_map/dot_general | solution.py:56
  15.1 0.0 reduce-scatter.3.cloned.1.call-update
  15.1 0.0 all-reduce.6.cloned.1.call-start
  15.2 0.9 copy-done.6
  16.1 0.2 copy.14
  16.3 0.0 copy-done.7
  16.4 11.0 %all_gather.20 = s32[256,256]{0,1:T(8,128)S(1)} all-gather(s32[256,64]{0,1:T(8,128)S(1)} %copy-done.7), channel_id=1, replica_groups=mesh['dp'=8,'rot'=4] {'rot'}, dimensions={1}, use_global_device_ids=true | all-gather | bytes 327680 | tf_op jit(solution)/shard_map/all_gather | solution.py:21
  27.4 0.1 pad_maximum_fusion.1
  27.5 1.8 collective-permute-start
  29.3 3.0 collective-permute-start.1
  32.3 1.2 collective-permute-start.2
  33.4 3.4 convert_reduce_fusion
  36.9 8.4 %collective-permute-done = bf16[256,1088]{0,1:T(8,128)(2,1)S(1)} collective-permute-done((bf16[256,1088]{0,1:T(8,128)(2,1)S(1)}, bf16[256,1088]{0,1:T(8,128)(2,1)S(1)}, u32[]{:S(2)}, u32[]{:S(2)}) %collective-permute-start) | collective-permute-done | bytes 557088 | tf_op jit(solution)/shard_map/ppermute | solution.py:45
  45.3 19.9 %collective-permute-done.1 = bf16[256,1088]{0,1:T(8,128)(2,1)S(1)} collective-permute-done((bf16[256,1088]{0,1:T(8,128)(2,1)S(1)}, bf16[256,1088]{0,1:T(8,128)(2,1)S(1)}, u32[]{:S(2)}, u32[]{:S(2)}) %collective-permute-start.1) | collective-permute-done | bytes 557088 | tf_op jit(solution)/shard_map/ppermute | solution.py:45
  65.2 0.0 collective-permute-done.2
  65.2 0.8 copy-done.1
  66.0 0.2 copy-done.2
  66.2 2.4 pad_maximum_fusion
  68.7 1.5 slice.21
  70.2 1.0 reduce-scatter.3.cloned.1.call-done
  71.2 1.3 convert_element_type.67
  72.5 5.1 fusion.3
  77.6 0.0 all-reduce.6.cloned.1.call-update
  77.6 0.0 all-gather.12.cloned.1.call-start
  77.7 4.2 fusion.17
  81.9 0.0 collective-permute-start.3
  81.9 64.6 %all-reduce.6.cloned.1.call-done = (f32[64,16,256]{2,1,0:T(8,128)}, f32[64,256]{1,0:T(8,128)}) async-done(((f32[64,16,256]{2,1,0:T(8,128)}, f32[64,256]{1,0:T(8,128)}), (f32[64,16,256]{2,1,0:T(8,128)}, f32[64,256]{1,0:T(8,128)})) %all-reduce.6.cloned.1.call-update) | async-done | bytes 1114128 | tf_op jit(solution)/shard_map/psum | solution.py:69
  146.5 0.8 broadcast_maximum_fusion
  147.3 1.3 broadcast_divide_fusion
  148.7 0.0 copy-start.3
  148.7 0.8 dynamic-slice_convert_fusion
  149.5 0.0 all-gather.12.cloned.1.call-update
  149.5 0.0 all-gather.6.cloned.1.call-start
  149.6 0.2 slice.20
  149.8 0.0 collective-permute-done.3
  149.8 0.9 fusion.18
  150.7 0.0 copy-done.3
  150.7 3.4 fusion.10
  154.1 21.1 %all-gather.12.cloned.1.call-done = bf16[128,16,256]{2,1,0:T(8,128)(2,1)} async-done(((bf16[32,16,256]{2,1,0:T(8,128)(2,1)}), bf16[128,16,256]{2,1,0:T(8,128)(2,1)}) %all-gather.12.cloned.1.call-update) | async-done | bytes 1048592 | tf_op jit(solution)/shard_map/all_gather | solution.py:76
  175.2 1.0 dynamic-slice_bitcast_fusion
  176.2 0.0 copy-start
  176.2 16.1 %fusion.11 = bf16[32,16,2048]{2,1,0:T(8,128)(2,1)S(1)} fusion(bf16[32,16,256]{2,1,0:T(8,128)(2,1)S(1)} %dynamic-slice_bitcast_fusion, s32[32,2048]{1,0:T(8,128)S(1)} %bitcast.25), kind=kOutput, calls=%fused_computation.19 | convolution fusion | flops 554696704 | bytes 2621440 | tf_op jit(solution)/shard_map/lyg,lxg->lyx/dot_general | solution.py:81
  192.3 3.3 convolution_convert_fusion.2
  195.6 0.0 all-gather.6.cloned.1.call-update
  195.6 0.2 reduce-scatter.5.cloned.1.call-start
  195.9 82.0 %all-gather.6.cloned.1.call-done = bf16[1024,4096]{1,0:T(8,128)(2,1)} async-done(((bf16[1024,512]{1,0:T(8,128)(2,1)}), bf16[1024,4096]{1,0:T(8,128)(2,1)}) %all-gather.6.cloned.1.call-update) | async-done | bytes 8388624 | tf_op jit(solution)/shard_map/all_gather | solution.py:99
  277.8 10.2 %convolution_convert_fusion.1 = bf16[4096,512]{1,0:T(8,128)(2,1)} fusion(bf16[1024,4096]{1,0:T(8,128)(2,1)} %all-gather.6.cloned.1.call-done, bf16[1024,512]{1,0:T(8,128)(2,1)} %convolution_convert_fusion.2), kind=kOutput, calls=%fused_computation.9 | convolution fusion | flops 4297064448 | bytes 13631488 | tf_op jit(solution)/shard_map/dot_general | solution.py:100
  288.0 0.0 reduce-scatter.5.cloned.1.call-update
  288.0 0.0 all-gather.8.cloned.1.call-start
  288.0 51.2 %reduce-scatter.5.cloned.1.call-done = bf16[1024,512]{1,0:T(8,128)(2,1)} async-done(((bf16[4096,512]{1,0:T(8,128)(2,1)}), bf16[1024,512]{1,0:T(8,128)(2,1)}) %reduce-scatter.5.cloned.1.call-update) | async-done | bytes 1048592 | tf_op jit(solution)/shard_map/reduce_scatter | solution.py:104
  339.2 0.0 all-gather.8.cloned.1.call-update
  339.3 0.0 all-gather.10.cloned.1.call-start
  339.3 2.4 multiply_reduce_fusion
  341.7 40.3 %psum.30 = f32[]{:T(128)} all-reduce(f32[]{:T(128)} %multiply_reduce_fusion), channel_id=1, replica_groups=mesh['dp'=8,'rot'=4] {'dp','rot'}, use_global_device_ids=true, to_apply=%region_6.7 | all-reduce | flops 1 | bytes 8 | tf_op jit(solution)/shard_map/psum | solution.py:109
  382.7 11.6 %all-gather.8.cloned.1.call-done = bf16[4096,512]{1,0:T(8,128)(2,1)} async-done(((bf16[1024,512]{1,0:T(8,128)(2,1)}), bf16[4096,512]{1,0:T(8,128)(2,1)}) %all-gather.8.cloned.1.call-update) | async-done | bytes 4194320 | tf_op jit(solution)/shard_map/all_gather | solution.py:92
  394.4 10.1 %multiply_convert_fusion.1 = bf16[1024,512]{1,0:T(8,128)(2,1)} fusion(bf16[1024,512]{1,0:T(8,128)(2,1)S(1)} %copy-done.4, bf16[1024,4096]{1,0:T(8,128)(2,1)} %all-gather.6.cloned.1.call-done, bf16[4096,512]{1,0:T(8,128)(2,1)} %all-gather.8.cloned.1.call-done, f32[]{:T(128)S(6)} %mul.79, f32[]{:T(128)S(6)} %div.24), kind=kOutput, calls=%fused_computation.28 | convolution fusion | flops 4298113024 | bytes 14680072 | tf_op jit(solution)/shard_map/dot_general | solution.py:90
  404.5 0.0 all-gather.10.cloned.1.call-update
  404.5 0.3 all-reduce.4.cloned.1.call-start
  404.7 81.9 %all-gather.10.cloned.1.call-done = bf16[1024,4096]{1,0:T(8,128)(2,1)} async-done(((bf16[1024,512]{1,0:T(8,128)(2,1)}), bf16[1024,4096]{1,0:T(8,128)(2,1)}) %all-gather.10.cloned.1.call-update) | async-done | bytes 8388624 | tf_op jit(solution)/shard_map/all_gather | solution.py:99
  486.7 10.1 %convolution_convert_fusion = bf16[4096,512]{1,0:T(8,128)(2,1)} fusion(bf16[1024,4096]{1,0:T(8,128)(2,1)} %all-gather.10.cloned.1.call-done, bf16[1024,512]{1,0:T(8,128)(2,1)} %multiply_convert_fusion.1), kind=kOutput, calls=%fused_computation.8 | convolution fusion | flops 4297064448 | bytes 13631488 | tf_op jit(solution)/shard_map/dot_general | solution.py:100
  496.8 0.0 all-reduce.4.cloned.1.call-update
  496.8 102.3 %all-reduce.4.cloned.1.call-done = bf16[4096,512]{1,0:T(8,128)(2,1)} async-done(((bf16[4096,512]{1,0:T(8,128)(2,1)}), bf16[4096,512]{1,0:T(8,128)(2,1)}) %all-reduce.4.cloned.1.call-update) | async-done | bytes 4194320 | tf_op jit(solution)/shard_map/psum | solution.py:106
  599.1 10.1 %multiply_convert_fusion = bf16[1024,512]{1,0:T(8,128)(2,1)} fusion(bf16[1024,512]{1,0:T(8,128)(2,1)S(1)} %copy-done.5, bf16[1024,4096]{1,0:T(8,128)(2,1)} %all-gather.10.cloned.1.call-done, bf16[4096,512]{1,0:T(8,128)(2,1)} %all-reduce.4.cloned.1.call-done), kind=kOutput, calls=%fused_computation.27 | convolution fusion | flops 4298113024 | bytes 14680064 | tf_op jit(solution)/shard_map/dot_general | solution.py:116
  (10 shorter events, 0.0 us)
Async XLA Ops:
  7.2 64.0 %reduce-scatter.3.cloned.1.call-start = ((), (), s32[]{:S(2)}) async-start(), calls=%async_computation.2 | async-start | bytes 5242880 | tf_op jit(solution)/shard_map/reduce_scatter | solution.py:55
  15.1 1.0 copy-start.6
  15.1 1.3 copy-start.7
  15.1 131.4 %all-reduce.6.cloned.1.call-start = ((), (), s32[]{:S(2)}) async-start(), calls=%async_computation.9 | async-start | bytes 2228224 | tf_op jit(solution)/shard_map/psum | solution.py:69
  27.5 17.8 %collective-permute-start = (bf16[256,1088]{0,1:T(8,128)(2,1)S(1)}, bf16[256,1088]{0,1:T(8,128)(2,1)S(1)}, u32[]{:S(2)}, u32[]{:S(2)}) collective-permute-start(bf16[256,1088]{0,1:T(8,128)(2,1)S(1)} %get-tuple-element.10), channel_id=1, source_target_pairs={{0,8},{4,12},{8,16},{12,20},{16,24},{20,28},{24,0},{28,4},{1,9},{5... | collective-permute-start | bytes 1671176 | tf_op jit(solution)/shard_map/ppermute | solution.py:45
  29.3 35.9 %collective-permute-start.1 = (bf16[256,1088]{0,1:T(8,128)(2,1)S(1)}, bf16[256,1088]{0,1:T(8,128)(2,1)S(1)}, u32[]{:S(2)}, u32[]{:S(2)}) collective-permute-start(bf16[256,1088]{0,1:T(8,128)(2,1)S(1)} %get-tuple-element.11), channel_id=1, source_target_pairs={{0,16},{4,20},{8,24},{12,28},{16,0},{20,4},{24,8},{28,12},{1,17},{... | collective-permute-start | bytes 1671176 | tf_op jit(solution)/shard_map/ppermute | solution.py:45
  32.3 33.0 %collective-permute-start.2 = (bf16[256,1088]{0,1:T(8,128)(2,1)S(1)}, bf16[256,1088]{0,1:T(8,128)(2,1)S(1)}, u32[]{:S(2)}, u32[]{:S(2)}) collective-permute-start(bf16[256,1088]{0,1:T(8,128)(2,1)S(1)} %get-tuple-element.12), channel_id=1, source_target_pairs={{0,24},{4,28},{8,0},{12,4},{16,8},{20,12},{24,16},{28,20},{1,25},{... | collective-permute-start | bytes 1671176 | tf_op jit(solution)/shard_map/ppermute | solution.py:45
  65.2 0.8 copy-start.1
  65.2 1.0 copy-start.2
  77.6 97.6 %all-gather.12.cloned.1.call-start = ((), (), s32[]{:S(2)}) async-start(), calls=%async_computation.8 | async-start | bytes 1310720 | tf_op jit(solution)/shard_map/all_gather | solution.py:76
  81.9 67.9 %collective-permute-start.3 = (bf16[1024,1056]{0,1:T(8,128)(2,1)}, bf16[1024,1056]{0,1:T(8,128)(2,1)}, u32[]{:S(2)}, u32[]{:S(2)}) collective-permute-start(bf16[1024,1056]{0,1:T(8,128)(2,1)} %fusion.17), channel_id=1, source_target_pairs={{0,4},{4,0},{8,12},{12,8},{16,20},{20,16},{24,28},{28,24},{1,5},{5... | collective-permute-start | bytes 6488072 | tf_op jit(solution)/shard_map/ppermute | solution.py:52
  148.7 2.0 copy-start.3
  149.5 128.3 %all-gather.6.cloned.1.call-start = ((), (), s32[]{:S(2)}) async-start(), calls=%async_computation.3 | async-start | bytes 9437184 | tf_op jit(solution)/shard_map/all_gather | solution.py:99
  176.2 16.1 %copy-start = (bf16[2048,1024]{0,1:T(8,128)(2,1)S(1)}, bf16[2048,1024]{0,1:T(8,128)(2,1)}, u32[]{:S(2)}) copy-start(bf16[2048,1024]{0,1:T(8,128)(2,1)} %fusion.10) | copy-start | bytes 12582916
  195.6 143.6 %reduce-scatter.5.cloned.1.call-start = ((), (), s32[]{:S(2)}) async-start(), calls=%async_computation.4 | async-start | bytes 5242880 | tf_op jit(solution)/shard_map/reduce_scatter | solution.py:104
  288.0 106.4 %copy-start.4 = (bf16[1024,512]{1,0:T(8,128)(2,1)S(1)}, bf16[1024,512]{1,0:T(8,128)(2,1)}, u32[]{:S(2)}) copy-start(bf16[1024,512]{1,0:T(8,128)(2,1)} %convolution_convert_fusion.2) | copy-start | bytes 3145732
  288.0 106.4 %all-gather.8.cloned.1.call-start = ((), (), s32[]{:S(2)}) async-start(), calls=%async_computation.5 | async-start | bytes 5242880 | tf_op jit(solution)/shard_map/all_gather | solution.py:92
  339.3 147.4 %all-gather.10.cloned.1.call-start = ((), (), s32[]{:S(2)}) async-start(), calls=%async_computation.6 | async-start | bytes 9437184 | tf_op jit(solution)/shard_map/all_gather | solution.py:99
  404.5 194.6 %all-reduce.4.cloned.1.call-start = ((), (), s32[]{:S(2)}) async-start(), calls=%async_computation.7 | async-start | bytes 8388608 | tf_op jit(solution)/shard_map/psum | solution.py:106
  496.8 102.3 %copy-start.5 = (bf16[1024,512]{1,0:T(8,128)(2,1)S(1)}, bf16[1024,512]{1,0:T(8,128)(2,1)}, u32[]{:S(2)}) copy-start(bf16[1024,512]{1,0:T(8,128)(2,1)} %multiply_convert_fusion.1) | copy-start | bytes 3145732
Sparse Core Ops, SparseCore 0:
  15.2 55.9 reduce-scatter.2
  77.7 68.7 all-reduce.5
  149.7 25.4 all-gather.11
  195.7 82.0 all-gather.5
  288.1 51.0 reduce-scatter.4
  340.9 53.3 all-gather.7
  404.6 82.0 all-gather.9
  496.9 102.0 all-reduce.3
where the time goes:
time: 616 us
  waiting for transfers between devices  444 us (72%)
  matrix products  72.8 us (12%)
  blocking collectives  51.3 us (8%)
  other arithmetic  20.3 us (3%)
  between operations  15.1 us (2%)
  starting transfers between devices  6.66 us (1%)
    all_gather x2, waiting for transfers between devices, body(): rows_b = lax.all_gather(columns, 'dp', axis=1, tiled=True)  164 us
    psum x1, waiting for transfers between devices, body(): gram_part = lax.psum(partial, 'rot')  102 us
    psum x1, waiting for transfers between devices, body(): total_sums, total_counts = lax.psum((shard_code_sums, local_counts), 'dp')  64.6 us
    reduce_scatter x1, waiting for transfers between devices, body(): lax.psum_scatter(partial, 'rot', scatter_dimension=0, tiled=True)  51.2 us
    psum x1, blocking collectives, body(): total = lax.psum(jnp.sum(gram_f * gram_f), ('dp', 'rot'))  40.3 us
    ppermute x3, waiting for transfers between devices, body(): lax.ppermute(pair_part((dp_index + shift) % dp_size), 'dp', pairs)  28.4 us
    all_gather x1, waiting for transfers between devices, body(): lax.all_gather(offered, 'rot', axis=0)[dp_index // blocks_per_rot]  21.1 us
    dot_general x2, matrix products, body(): lax.dot_general(rows_b, columns, (((0,), (0,)), ((), ())), preferred_elem...  20.3 us
  transfers between devices with their start and end apart: 12, of which 10 were waited for; matrix products, arithmetic and copies ran while one was open for 4% of the time, Pallas kernels for 0%

commit v1 on v0

--- a/solution.py
+++ b/solution.py
@@ -103,7 +103,7 @@
         if iteration == 0:
             gram_part = lax.psum_scatter(partial, "rot", scatter_dimension=0, tiled=True)
         else:
-            gram_part = lax.psum(partial, "rot")
+            gram_part = jnp.sum(lax.all_gather(partial, "rot"), axis=0)
         if iteration == 0:
             gram_f = gram_part.astype(jnp.float32)
             total = lax.psum(jnp.sum(gram_f * gram_f), ("dp", "rot"))

time: 616 us -> 682 us (1.11)
  waiting for transfers between devices: 444 us -> 498 us
  other arithmetic: 20.3 us -> 32.1 us
    all_gather x0 -> x1, waiting for transfers between devices: none -> 156 us  [body(): gram_part = jnp.sum(lax.all_gather(partial, 'rot'), axis=0)]
    psum x1 -> x0, waiting for transfers between devices: 102 us -> none  [body(): gram_part = lax.psum(partial, 'rot')]
    reduce_sum x0 -> x1, other arithmetic: none -> 11.8 us  [body(): gram_part = jnp.sum(lax.all_gather(partial, 'rot'), axis=0)]
  transfers between devices with their start and end apart: 12 -> 12, of which waited for: 10 -> 10; matrix products, arithmetic and copies ran while one was open for 4% -> 3% of each run, Pallas kernels for 0% -> 0%
where the time goes in v1:
time: 682 us
  waiting for transfers between devices  498 us (73%)
  matrix products  72.9 us (11%)
  blocking collectives  51.4 us (8%)
  other arithmetic  32.1 us (5%)
  between operations  15.1 us (2%)
    all_gather x2, waiting for transfers between devices, body(): rows_b = lax.all_gather(columns, 'dp', axis=1, tiled=True)  164 us
    all_gather x1, waiting for transfers between devices, body(): gram_part = jnp.sum(lax.all_gather(partial, 'rot'), axis=0)  156 us
    psum x1, waiting for transfers between devices, body(): total_sums, total_counts = lax.psum((shard_code_sums, local_counts), 'dp')  64.6 us
    reduce_scatter x1, waiting for transfers between devices, body(): lax.psum_scatter(partial, 'rot', scatter_dimension=0, tiled=True)  51.2 us
    psum x1, blocking collectives, body(): total = lax.psum(jnp.sum(gram_f * gram_f), ('dp', 'rot'))  40.4 us
    ppermute x3, waiting for transfers between devices, body(): lax.ppermute(pair_part((dp_index + shift) % dp_size), 'dp', pairs)  28.4 us
    all_gather x1, waiting for transfers between devices, body(): lax.all_gather(offered, 'rot', axis=0)[dp_index // blocks_per_rot]  21.1 us
    dot_general x2, matrix products, body(): lax.dot_general(rows_b, columns, (((0,), (0,)), ((), ())), preferred_elem...  20.3 us
  transfers between devices with their start and end apart: 12, of which 10 were waited for; matrix products, arithmetic and copies ran while one was open for 3% of the time, Pallas kernels for 0%

profile of v1, /device:TPU:0, one launch (start us, length us, event | category | flops | bytes accessed | tf_op | source)
XLA Modules:
  0.0 681.5 jit_solution(14553981289793590363)
XLA Ops:
  7.2 0.0 reduce-scatter.3.cloned.1.call-start
  7.2 7.8 %fusion.19 = f32[4096,256]{1,0:T(8,128)} fusion(bf16[1024,4096]{1,0:T(8,128)(2,1)} %param.4, bf16[256,1024]{1,0:T(8,128)(2,1)} %param.3), kind=kOutput, calls=%fused_computation.48 | convolution fusion | flops 2147483648 | bytes 13107200 | tf_op jit(solution)/shard_map/dot_general | solution.py:56
  15.1 0.0 reduce-scatter.3.cloned.1.call-update
  15.1 0.0 all-reduce.3.cloned.1.call-start
  15.2 0.9 copy-done.6
  16.1 0.2 copy.14
  16.3 0.0 copy-done.7
  16.4 11.0 %all_gather.26 = s32[256,256]{0,1:T(8,128)S(1)} all-gather(s32[256,64]{0,1:T(8,128)S(1)} %copy-done.7), channel_id=1, replica_groups=mesh['dp'=8,'rot'=4] {'rot'}, dimensions={1}, use_global_device_ids=true | all-gather | bytes 327680 | tf_op jit(solution)/shard_map/all_gather | solution.py:21
  27.4 0.1 pad_maximum_fusion.1
  27.5 1.8 collective-permute-start
  29.3 3.0 collective-permute-start.1
  32.3 1.2 collective-permute-start.2
  33.4 3.4 convert_reduce_fusion
  36.9 8.4 %collective-permute-done = bf16[256,1088]{0,1:T(8,128)(2,1)S(1)} collective-permute-done((bf16[256,1088]{0,1:T(8,128)(2,1)S(1)}, bf16[256,1088]{0,1:T(8,128)(2,1)S(1)}, u32[]{:S(2)}, u32[]{:S(2)}) %collective-permute-start) | collective-permute-done | bytes 557088 | tf_op jit(solution)/shard_map/ppermute | solution.py:45
  45.3 19.9 %collective-permute-done.1 = bf16[256,1088]{0,1:T(8,128)(2,1)S(1)} collective-permute-done((bf16[256,1088]{0,1:T(8,128)(2,1)S(1)}, bf16[256,1088]{0,1:T(8,128)(2,1)S(1)}, u32[]{:S(2)}, u32[]{:S(2)}) %collective-permute-start.1) | collective-permute-done | bytes 557088 | tf_op jit(solution)/shard_map/ppermute | solution.py:45
  65.2 0.0 collective-permute-done.2
  65.2 0.8 copy-done.1
  66.0 0.2 copy-done.2
  66.2 2.4 pad_maximum_fusion
  68.7 1.5 slice.21
  70.2 1.0 reduce-scatter.3.cloned.1.call-done
  71.2 1.3 convert_element_type.69
  72.5 5.1 fusion.3
  77.6 0.0 all-reduce.3.cloned.1.call-update
  77.6 0.0 all-gather.14.cloned.1.call-start
  77.7 4.2 fusion.17
  81.9 0.0 collective-permute-start.3
  81.9 64.6 %all-reduce.3.cloned.1.call-done = (f32[64,16,256]{2,1,0:T(8,128)}, f32[64,256]{1,0:T(8,128)}) async-done(((f32[64,16,256]{2,1,0:T(8,128)}, f32[64,256]{1,0:T(8,128)}), (f32[64,16,256]{2,1,0:T(8,128)}, f32[64,256]{1,0:T(8,128)})) %all-reduce.3.cloned.1.call-update) | async-done | bytes 1114128 | tf_op jit(solution)/shard_map/psum | solution.py:69
  146.5 0.8 broadcast_maximum_fusion
  147.3 1.3 broadcast_divide_fusion
  148.7 0.0 copy-start.3
  148.7 0.8 dynamic-slice_convert_fusion
  149.5 0.0 all-gather.14.cloned.1.call-update
  149.5 0.0 all-gather.8.cloned.1.call-start
  149.6 0.2 slice.20
  149.8 0.0 collective-permute-done.3
  149.8 0.9 fusion.18
  150.7 3.4 fusion.10
  154.1 21.1 %all-gather.14.cloned.1.call-done = bf16[128,16,256]{2,1,0:T(8,128)(2,1)} async-done(((bf16[32,16,256]{2,1,0:T(8,128)(2,1)}), bf16[128,16,256]{2,1,0:T(8,128)(2,1)}) %all-gather.14.cloned.1.call-update) | async-done | bytes 1048592 | tf_op jit(solution)/shard_map/all_gather | solution.py:76
  175.2 1.0 dynamic-slice_bitcast_fusion
  176.2 16.1 %fusion.11 = bf16[32,16,2048]{2,1,0:T(8,128)(2,1)S(1)} fusion(bf16[32,16,256]{2,1,0:T(8,128)(2,1)S(1)} %dynamic-slice_bitcast_fusion, s32[32,2048]{1,0:T(8,128)S(1)} %bitcast.27), kind=kOutput, calls=%fused_computation.19 | convolution fusion | flops 554696704 | bytes 2621440 | tf_op jit(solution)/shard_map/lyg,lxg->lyx/dot_general | solution.py:81
  192.2 0.0 copy-done
  192.3 3.3 convolution_convert_fusion.2
  195.6 0.0 all-gather.8.cloned.1.call-update
  195.6 0.2 reduce-scatter.5.cloned.1.call-start
  195.8 82.0 %all-gather.8.cloned.1.call-done = bf16[1024,4096]{1,0:T(8,128)(2,1)} async-done(((bf16[1024,512]{1,0:T(8,128)(2,1)}), bf16[1024,4096]{1,0:T(8,128)(2,1)}) %all-gather.8.cloned.1.call-update) | async-done | bytes 8388624 | tf_op jit(solution)/shard_map/all_gather | solution.py:99
  277.8 10.2 %convolution_convert_fusion.1 = bf16[4096,512]{1,0:T(8,128)(2,1)} fusion(bf16[1024,4096]{1,0:T(8,128)(2,1)} %all-gather.8.cloned.1.call-done, bf16[1024,512]{1,0:T(8,128)(2,1)} %convolution_convert_fusion.2), kind=kOutput, calls=%fused_computation.9 | convolution fusion | flops 4297064448 | bytes 13631488 | tf_op jit(solution)/shard_map/dot_general | solution.py:100
  288.0 0.0 reduce-scatter.5.cloned.1.call-update
  288.0 0.0 all-gather.10.cloned.1.call-start
  288.0 51.2 %reduce-scatter.5.cloned.1.call-done = bf16[1024,512]{1,0:T(8,128)(2,1)} async-done(((bf16[4096,512]{1,0:T(8,128)(2,1)}), bf16[1024,512]{1,0:T(8,128)(2,1)}) %reduce-scatter.5.cloned.1.call-update) | async-done | bytes 1048592 | tf_op jit(solution)/shard_map/reduce_scatter | solution.py:104
  339.2 0.0 all-gather.10.cloned.1.call-update
  339.3 0.0 all-gather.12.cloned.1.call-start
  339.3 2.4 multiply_reduce_fusion
  341.7 40.4 %psum.23 = f32[]{:T(128)} all-reduce(f32[]{:T(128)} %multiply_reduce_fusion), channel_id=1, replica_groups=mesh['dp'=8,'rot'=4] {'dp','rot'}, use_global_device_ids=true, to_apply=%region_6.7 | all-reduce | flops 1 | bytes 8 | tf_op jit(solution)/shard_map/psum | solution.py:109
  382.8 11.5 %all-gather.10.cloned.1.call-done = bf16[4096,512]{1,0:T(8,128)(2,1)} async-done(((bf16[1024,512]{1,0:T(8,128)(2,1)}), bf16[4096,512]{1,0:T(8,128)(2,1)}) %all-gather.10.cloned.1.call-update) | async-done | bytes 4194320 | tf_op jit(solution)/shard_map/all_gather | solution.py:92
  394.3 10.1 %multiply_convert_fusion.1 = bf16[1024,512]{1,0:T(8,128)(2,1)} fusion(bf16[1024,512]{1,0:T(8,128)(2,1)S(1)} %copy-done.4, bf16[1024,4096]{1,0:T(8,128)(2,1)} %all-gather.8.cloned.1.call-done, bf16[4096,512]{1,0:T(8,128)(2,1)} %all-gather.10.cloned.1.call-done, f32[]{:T(128)S(6)} %mul.79, f32[]{:T(128)S(6)} %div.24), kind=kOutput, calls=%fused_computation.28 | convolution fusion | flops 4298113024 | bytes 14680072 | tf_op jit(solution)/shard_map/dot_general | solution.py:90
  404.4 0.0 all-gather.12.cloned.1.call-update
  404.4 0.3 all-gather.16.cloned.1.call-start
  404.7 81.9 %all-gather.12.cloned.1.call-done = bf16[1024,4096]{1,0:T(8,128)(2,1)} async-done(((bf16[1024,512]{1,0:T(8,128)(2,1)}), bf16[1024,4096]{1,0:T(8,128)(2,1)}) %all-gather.12.cloned.1.call-update) | async-done | bytes 8388624 | tf_op jit(solution)/shard_map/all_gather | solution.py:99
  486.6 10.2 %convolution_convert_fusion = bf16[4096,512]{1,0:T(8,128)(2,1)} fusion(bf16[1024,4096]{1,0:T(8,128)(2,1)} %all-gather.12.cloned.1.call-done, bf16[1024,512]{1,0:T(8,128)(2,1)} %multiply_convert_fusion.1), kind=kOutput, calls=%fused_computation.8 | convolution fusion | flops 4297064448 | bytes 13631488 | tf_op jit(solution)/shard_map/dot_general | solution.py:100
  496.8 0.0 all-gather.16.cloned.1.call-update
  496.8 155.9 %all-gather.16.cloned.1.call-done = bf16[16384,512]{1,0:T(8,128)(2,1)} async-done(((bf16[4096,512]{1,0:T(8,128)(2,1)}), bf16[16384,512]{1,0:T(8,128)(2,1)}) %all-gather.16.cloned.1.call-update) | async-done | bytes 16777232 | tf_op jit(solution)/shard_map/all_gather | solution.py:106
  652.8 11.8 %reduce_sum.32 = bf16[4096,512]{1,0:T(8,128)(2,1)} reduce(bf16[4,4096,512]{2,1,0:T(8,128)(2,1)} %bitcast.24, bf16[]{:T(256)} %constant.75.clone.1), dimensions={0}, to_apply=%region_7.8 | reduce | flops 6291456 | bytes 20971522 | tf_op jit(solution)/shard_map/reduce_sum | solution.py:106
  664.6 10.1 %multiply_convert_fusion = bf16[1024,512]{1,0:T(8,128)(2,1)} fusion(bf16[1024,512]{1,0:T(8,128)(2,1)S(1)} %copy-done.5, bf16[1024,4096]{1,0:T(8,128)(2,1)} %all-gather.12.cloned.1.call-done, bf16[4096,512]{1,0:T(8,128)(2,1)} %reduce_sum.32), kind=kOutput, calls=%fused_computation.27 | convolution fusion | flops 4298113024 | bytes 14680064 | tf_op jit(solution)/shard_map/dot_general | solution.py:116
  (11 shorter events, 0.0 us)
Async XLA Ops:
  7.2 64.0 %reduce-scatter.3.cloned.1.call-start = ((), (), s32[]{:S(2)}) async-start(), calls=%async_computation.2 | async-start | bytes 5242880 | tf_op jit(solution)/shard_map/reduce_scatter | solution.py:55
  15.1 1.0 copy-start.6
  15.1 1.3 copy-start.7
  15.1 131.4 %all-reduce.3.cloned.1.call-start = ((), (), s32[]{:S(2)}) async-start(), calls=%async_computation.9 | async-start | bytes 2228224 | tf_op jit(solution)/shard_map/psum | solution.py:69
  27.5 17.8 %collective-permute-start = (bf16[256,1088]{0,1:T(8,128)(2,1)S(1)}, bf16[256,1088]{0,1:T(8,128)(2,1)S(1)}, u32[]{:S(2)}, u32[]{:S(2)}) collective-permute-start(bf16[256,1088]{0,1:T(8,128)(2,1)S(1)} %get-tuple-element.10), channel_id=1, source_target_pairs={{0,8},{4,12},{8,16},{12,20},{16,24},{20,28},{24,0},{28,4},{1,9},{5... | collective-permute-start | bytes 1671176 | tf_op jit(solution)/shard_map/ppermute | solution.py:45
  29.3 35.9 %collective-permute-start.1 = (bf16[256,1088]{0,1:T(8,128)(2,1)S(1)}, bf16[256,1088]{0,1:T(8,128)(2,1)S(1)}, u32[]{:S(2)}, u32[]{:S(2)}) collective-permute-start(bf16[256,1088]{0,1:T(8,128)(2,1)S(1)} %get-tuple-element.11), channel_id=1, source_target_pairs={{0,16},{4,20},{8,24},{12,28},{16,0},{20,4},{24,8},{28,12},{1,17},{... | collective-permute-start | bytes 1671176 | tf_op jit(solution)/shard_map/ppermute | solution.py:45
  32.3 33.0 %collective-permute-start.2 = (bf16[256,1088]{0,1:T(8,128)(2,1)S(1)}, bf16[256,1088]{0,1:T(8,128)(2,1)S(1)}, u32[]{:S(2)}, u32[]{:S(2)}) collective-permute-start(bf16[256,1088]{0,1:T(8,128)(2,1)S(1)} %get-tuple-element.12), channel_id=1, source_target_pairs={{0,24},{4,28},{8,0},{12,4},{16,8},{20,12},{24,16},{28,20},{1,25},{... | collective-permute-start | bytes 1671176 | tf_op jit(solution)/shard_map/ppermute | solution.py:45
  65.2 0.8 copy-start.1
  65.2 1.0 copy-start.2
  77.6 97.6 %all-gather.14.cloned.1.call-start = ((), (), s32[]{:S(2)}) async-start(), calls=%async_computation.7 | async-start | bytes 1310720 | tf_op jit(solution)/shard_map/all_gather | solution.py:76
  81.9 67.9 %collective-permute-start.3 = (bf16[1024,1056]{0,1:T(8,128)(2,1)}, bf16[1024,1056]{0,1:T(8,128)(2,1)}, u32[]{:S(2)}, u32[]{:S(2)}) collective-permute-start(bf16[1024,1056]{0,1:T(8,128)(2,1)} %fusion.17), channel_id=1, source_target_pairs={{0,4},{4,0},{8,12},{12,8},{16,20},{20,16},{24,28},{28,24},{1,5},{5... | collective-permute-start | bytes 6488072 | tf_op jit(solution)/shard_map/ppermute | solution.py:52
  148.7 2.0 copy-start.3
  149.5 128.3 %all-gather.8.cloned.1.call-start = ((), (), s32[]{:S(2)}) async-start(), calls=%async_computation.3 | async-start | bytes 9437184 | tf_op jit(solution)/shard_map/all_gather | solution.py:99
  176.1 16.1 %copy-start = (bf16[2048,1024]{0,1:T(8,128)(2,1)S(1)}, bf16[2048,1024]{0,1:T(8,128)(2,1)}, u32[]{:S(2)}) copy-start(bf16[2048,1024]{0,1:T(8,128)(2,1)} %fusion.10) | copy-start | bytes 12582916
  195.6 143.6 %reduce-scatter.5.cloned.1.call-start = ((), (), s32[]{:S(2)}) async-start(), calls=%async_computation.4 | async-start | bytes 5242880 | tf_op jit(solution)/shard_map/reduce_scatter | solution.py:104
  288.0 106.4 %copy-start.4 = (bf16[1024,512]{1,0:T(8,128)(2,1)S(1)}, bf16[1024,512]{1,0:T(8,128)(2,1)}, u32[]{:S(2)}) copy-start(bf16[1024,512]{1,0:T(8,128)(2,1)} %convolution_convert_fusion.2) | copy-start | bytes 3145732
  288.0 106.3 %all-gather.10.cloned.1.call-start = ((), (), s32[]{:S(2)}) async-start(), calls=%async_computation.5 | async-start | bytes 5242880 | tf_op jit(solution)/shard_map/all_gather | solution.py:92
  339.3 147.4 %all-gather.12.cloned.1.call-start = ((), (), s32[]{:S(2)}) async-start(), calls=%async_computation.6 | async-start | bytes 9437184 | tf_op jit(solution)/shard_map/all_gather | solution.py:99
  404.4 248.3 %all-gather.16.cloned.1.call-start = ((), (), s32[]{:S(2)}) async-start(), calls=%async_computation.8 | async-start | bytes 20971520 | tf_op jit(solution)/shard_map/all_gather | solution.py:106
  652.8 11.8 %copy-start.5 = (bf16[1024,512]{1,0:T(8,128)(2,1)S(1)}, bf16[1024,512]{1,0:T(8,128)(2,1)}, u32[]{:S(2)}) copy-start(bf16[1024,512]{1,0:T(8,128)(2,1)} %multiply_convert_fusion.1) | copy-start | bytes 3145732
Sparse Core Ops, SparseCore 0:
  15.2 55.9 reduce-scatter.2
  77.7 68.7 all-reduce.2
  149.6 25.4 all-gather.13
  195.7 82.0 all-gather.7
  288.1 51.0 reduce-scatter.4
  340.9 53.3 all-gather.9
  404.6 82.0 all-gather.11
  496.9 155.7 all-gather.15
